TPU v7x, 256 devices: a whole 4x4x8 slice. The times are simulated.
256 devices in a mesh: dp: 32 (over x_lo, z, core), tensor: 8 (over x_hi, y).
Axes of the slice: x: 4 (x_hi: 2, x_lo: 2; x = x_hi * 2 + x_lo), y: 4, z: 8, core: 2. Of those that a mesh axis runs over, the one named last changes fastest.
Arguments:
- hidden_input_state: bfloat16 [12288, 4608], P('dp', 'tensor'), may hold values from -80 to 80
- norm_gain: float32 [4608], replicated, may hold values from 0.5 to 1.5
- head_weight: bfloat16 [4608, 8192], P(None, 'tensor'), may hold values from -2 to 2
- target_ids: int32 [12288], P('dp'), may hold values from 0 to 8191
Outputs:
- hidden_state_gradient: float32 [12288, 4608], P('dp', 'tensor')
- grad_head: float32 [4608, 8192], P('dp', 'tensor')
- norm_gain_gradient: float32 [4608], P('tensor')
All inputs are finite; a program needn't handle non-finite values.
Results may differ from a plain program's by a relative error of at most 0.0039.
Values may be sent and summed in bfloat16 or wider, within the bound.
No kernel may reach another device: no remote copies, remote signals or barrier semaphores. Data moves between devices by JAX's collectives and lax.ppermute only.
A program may use at most 192 MiB of HBM per device.

v0:
```python
import jax
import jax.numpy as jnp
import numpy as np
from jax import lax
from jax.sharding import PartitionSpec as P

epsilon = 1e-06


def ring_order(n_hi, n_lo):
    order = []
    for hi in range(n_hi):
        los = range(n_lo) if hi % 2 == 0 else range(n_lo - 1, -1, -1)
        order += [hi * n_lo + lo for lo in los]
    return order


def ring_reduce_scatter(fwd, bwd, axis, order):
    n = len(order)
    pos_of = np.zeros(n, np.int32)
    for p, t in enumerate(order):
        pos_of[t] = p
    order_arr = jnp.asarray(np.asarray(order, np.int32))
    me = lax.axis_index(axis)
    pos = jnp.asarray(pos_of)[me]
    perm_f = [(order[p], order[(p + 1) % n]) for p in range(n)]
    perm_b = [(order[p], order[(p - 1) % n]) for p in range(n)]
    recv_f = recv_b = None
    for s in range(n - 1):
        qf = order_arr[(pos - 1 - s) % n]
        qb = order_arr[(pos + 1 + s) % n]
        send_f = lax.dynamic_index_in_dim(fwd, qf, 0, keepdims=False)
        send_b = lax.dynamic_index_in_dim(bwd, qb, 0, keepdims=False)
        if recv_f is not None:
            send_f = send_f + recv_f
            send_b = send_b + recv_b
        recv_f = lax.ppermute(send_f, axis, perm_f)
        recv_b = lax.ppermute(send_b, axis, perm_b)
    own_f = lax.dynamic_index_in_dim(fwd, me, 0, keepdims=False)
    own_b = lax.dynamic_index_in_dim(bwd, me, 0, keepdims=False)
    return (own_f + recv_f, own_b + recv_b)


def shards(hidden_input_state, norm_gain, head_weight, target_ids):
    tokens, local_cols = hidden_input_state.shape
    width, vocab_rows = head_weight.shape
    n_tensor = width // local_cols
    gathered = lax.all_gather(hidden_input_state, "tensor", axis=1, tiled=True)
    values = gathered.astype(jnp.float32)
    scaled_rows = lax.rsqrt(jnp.mean(values * values, axis=1, keepdims=True) + epsilon)
    normalized = values * scaled_rows
    normed = (normalized * norm_gain[None, :]).astype(jnp.bfloat16)
    logits = jnp.dot(normed, head_weight, preferred_element_type=jnp.float32)
    local_top = jnp.max(logits, axis=1)
    local_total = jnp.sum(jnp.exp(logits - local_top[:, None]), axis=1)
    stats = lax.all_gather(jnp.stack([local_top, local_total]), "tensor", axis=0)
    row_top = jnp.max(stats[:, 0, :], axis=0)
    row_total = jnp.sum(stats[:, 1, :] * jnp.exp(stats[:, 0, :] - row_top[None, :]), axis=0)
    log_total = row_top + jnp.log(row_total)
    offset = lax.axis_index("tensor") * vocab_rows
    column_ids = offset + lax.broadcasted_iota(jnp.int32, (1, vocab_rows), 1)
    onehot = (column_ids == target_ids[:, None]).astype(jnp.float32)
    dlogits = (jnp.exp(logits - log_total[:, None]) - onehot).astype(jnp.bfloat16)
    grad_head = lax.psum_scatter(
        lax.dot_general(
            normed, dlogits, (((0,), (0,)), ((), ())), preferred_element_type=jnp.float32
        ),
        "dp",
        scatter_dimension=0,
        tiled=True,
    )
    partial = lax.dot_general(
        head_weight, dlogits, (((1,), (1,)), ((), ())), preferred_element_type=jnp.float32
    )
    inner_part = jnp.sum(partial * (norm_gain[:, None] * normalized.T), axis=0)
    chunks = partial.reshape(n_tensor, local_cols, tokens)
    half = local_cols // 2
    extra = (
        jnp.zeros((n_tensor, 8, tokens), jnp.float32)
        .at[:, 0, :]
        .set(jnp.broadcast_to(inner_part[None, :], (n_tensor, tokens)))
    )
    fwd = jnp.concatenate([chunks[:, :half, :], extra], axis=1)
    bwd = chunks[:, half:, :]
    order = ring_order(2, n_tensor // 2)
    got_f, got_b = ring_reduce_scatter(fwd, bwd, "tensor", order)
    grad_cols = jnp.concatenate([got_f[:half], got_b], axis=0)
    row_inner_sum = got_f[half] / width
    normed_gradient = grad_cols.T
    start_col = lax.axis_index("tensor") * local_cols
    normalized_slice = hidden_input_state.astype(jnp.float32) * scaled_rows
    gain_slice = lax.dynamic_slice_in_dim(norm_gain, start_col, local_cols)
    weighted_rows = normed_gradient * gain_slice[None, :]
    hidden_state_gradient = scaled_rows * (
        weighted_rows - normalized_slice * row_inner_sum[:, None]
    )
    norm_gain_gradient = lax.psum(jnp.sum(normed_gradient * normalized_slice, axis=0), "dp")
    return (hidden_state_gradient, grad_head, norm_gain_gradient)


def solution(mesh):
    return jax.shard_map(
        shards,
        mesh=mesh,
        in_specs=(P("dp", "tensor"), P(), P(None, "tensor"), P("dp")),
        out_specs=(P("dp", "tensor"), P("dp", "tensor"), P("tensor")),
        check_vma=False,
    )
```

profile of v0, /device:TPU:1, one launch (start us, length us, event | category | flops | bytes accessed | tf_op | source)
XLA Modules:
  0.0 408.9 jit_solution(1212143429641370767)
XLA Ops:
  8.0 77.0 %all-gather.4.cloned.1.call-done = bf16[384,4608]{0,1:T(8,128)(2,1)} async-done(((bf16[384,576]{0,1:T(8,128)(2,1)}), bf16[384,4608]{0,1:T(8,128)(2,1)}) %all-gather.4.cloned.1.call-update) | async-done | bytes 3538960 | tf_op jit(solution)/shard_map/all_gather | solution.py:48
  85.0 4.3 %copy.30 = bf16[384,4608]{1,0:T(8,128)(2,1)S(1)} copy(bf16[384,4608]{0,1:T(8,128)(2,1)} %all-gather.4.cloned.1.call-done) | data formatting | bytes 7077888 | tf_op jit(solution)/shard_map/all_gather | solution.py:48
  90.1 6.6 %fusion.17 = (f32[384]{0:T(512)S(1)}, f32[384,1024]{1,0:T(8,128)S(1)}) fusion(bf16[4608,1024]{1,0:T(8,128)(2,1)} %param.10, bf16[384,4608]{1,0:T(8,128)(2,1)S(1)} %copy.30, f32[4608]{0:T(1024)S(1)} %copy-done.6, f32[384]{0:T(512)S(1)} %add_rsqrt_fusion), kind=kOutput, calls=%fused_computation.50 | convolution fusion | flops 3631349248 | bytes 14570496 | tf_op jit(solution)/shard_map/dot_general | solution.py:53
  97.2 27.8 %all-gather.1 = f32[8,2,384]{2,1,0:T(2,128)S(1)} all-gather(f32[1,2,384]{2,1,0:T(2,128)S(1)} %maximum_bitcast_fusion.1), channel_id=2, replica_groups=mesh['dp'=32,'tensor'=8] {'tensor'}, dimensions={0}, use_global_device_ids=true | all-gather | bytes 27648 | tf_op jit(solution)/shard_map/all_gather | solution.py:56
  125.1 9.5 %fusion.6 = f32[4608,1024]{1,0:T(8,128)} fusion(bf16[384,4608]{1,0:T(8,128)(2,1)S(1)} %copy.30, f32[4608]{0:T(1024)S(1)} %copy-done.6, f32[384]{0:T(512)S(1)} %add_rsqrt_fusion, f32[384,1024]{1,0:T(8,128)S(1)} %get-tuple-element.37, s32[1024]{0:T(1024)S(1)} %iota_add_fusion, f32[384]{0:T(512)S(1)} %log_add_fusion, s32[384]{0:T(512)S(1)} %copy-done.7), kind=kOutput, calls=%fused_computation.13 | convolution fusion | flops 3632922624 | bytes 24013312 | tf_op jit(solution)/shard_map/dot_general | solution.py:65
  149.5 11.5 %fusion.5 = (f32[384]{0:T(512)S(1)}, f32[4608,384]{0,1:T(8,128)}) fusion(bf16[384,4608]{1,0:T(8,128)(2,1)S(1)} %copy.30, f32[4608]{0:T(1024)} %param.9, f32[384]{0:T(512)S(1)} %add_rsqrt_fusion, bf16[4608,1024]{1,0:T(8,128)(2,1)} %param.10, f32[384,1024]{1,0:T(8,128)} %copy-done.3, s32[1024]{0:T(1024)S(1)} %iota_add_fusion, f32[384]{0:T(512)S(1)} %log_add_fusion, ...), kind=kOutput, calls=%fused_computation.8 | convolution fusion | flops 3634691584 | bytes 21655552 | tf_op jit(solution)/shard_map/dot_general | solution.py:72
  161.0 8.1 %copy.32 = f32[4608,384]{1,0:T(8,128)} copy(f32[4608,384]{0,1:T(8,128)} %get-tuple-element.39) | data formatting | bytes 14155776 | tf_op jit(solution)/shard_map/dot_general | solution.py:72
  169.1 3.7 fusion.14
  182.4 16.3 %collective-permute-done.7 = f32[288,384]{1,0:T(8,128)} collective-permute-done((f32[288,384]{1,0:T(8,128)}, f32[288,384]{1,0:T(8,128)}, u32[]{:S(2)}, u32[]{:S(2)}) %collective-permute-start.7) | collective-permute-done | bytes 442400 | tf_op jit(solution)/shard_map/ppermute | solution.py:38
  198.7 2.0 bitcast_add_fusion.7
  200.7 7.0 %collective-permute-start.8 = (f32[288,384]{1,0:T(8,128)}, f32[288,384]{1,0:T(8,128)}, u32[]{:S(2)}, u32[]{:S(2)}) collective-permute-start(f32[288,384]{1,0:T(8,128)} %bitcast_add_fusion.7), channel_id=1, source_target_pairs={{0,4},{1,0},{2,1},{3,2},{7,3},{6,7},{5,6},{4,5},{8,12},{9,8},{10,9... | collective-permute-start | bytes 1327112 | tf_op jit(solution)/shard_map/ppermute | solution.py:38
  207.7 7.3 %collective-permute-done = f32[296,384]{1,0:T(8,128)} collective-permute-done((f32[296,384]{1,0:T(8,128)}, f32[296,384]{1,0:T(8,128)}, u32[]{:S(2)}, u32[]{:S(2)}) %collective-permute-start) | collective-permute-done | bytes 454688 | tf_op jit(solution)/shard_map/ppermute | solution.py:37
  215.0 2.0 bitcast_add_fusion
  220.7 10.4 %collective-permute-done.8 = f32[288,384]{1,0:T(8,128)} collective-permute-done((f32[288,384]{1,0:T(8,128)}, f32[288,384]{1,0:T(8,128)}, u32[]{:S(2)}, u32[]{:S(2)}) %collective-permute-start.8) | collective-permute-done | bytes 442400 | tf_op jit(solution)/shard_map/ppermute | solution.py:38
  231.1 2.0 bitcast_add_fusion.8
  233.1 6.2 %collective-permute-start.9 = (f32[288,384]{1,0:T(8,128)}, f32[288,384]{1,0:T(8,128)}, u32[]{:S(2)}, u32[]{:S(2)}) collective-permute-start(f32[288,384]{1,0:T(8,128)} %bitcast_add_fusion.8), channel_id=1, source_target_pairs={{0,4},{1,0},{2,1},{3,2},{7,3},{6,7},{5,6},{4,5},{8,12},{9,8},{10,9... | collective-permute-start | bytes 1327112 | tf_op jit(solution)/shard_map/ppermute | solution.py:38
  239.3 10.3 %collective-permute-done.1 = f32[296,384]{1,0:T(8,128)} collective-permute-done((f32[296,384]{1,0:T(8,128)}, f32[296,384]{1,0:T(8,128)}, u32[]{:S(2)}, u32[]{:S(2)}) %collective-permute-start.1) | collective-permute-done | bytes 454688 | tf_op jit(solution)/shard_map/ppermute | solution.py:37
  249.6 2.0 bitcast_add_fusion.1
  255.1 18.2 %collective-permute-done.9 = f32[288,384]{1,0:T(8,128)} collective-permute-done((f32[288,384]{1,0:T(8,128)}, f32[288,384]{1,0:T(8,128)}, u32[]{:S(2)}, u32[]{:S(2)}) %collective-permute-start.9) | collective-permute-done | bytes 442400 | tf_op jit(solution)/shard_map/ppermute | solution.py:38
  275.2 3.8 collective-permute-start.10
  279.0 5.7 %collective-permute-done.2 = f32[296,384]{1,0:T(8,128)} collective-permute-done((f32[296,384]{1,0:T(8,128)}, f32[296,384]{1,0:T(8,128)}, u32[]{:S(2)}, u32[]{:S(2)}) %collective-permute-start.2) | collective-permute-done | bytes 454688 | tf_op jit(solution)/shard_map/ppermute | solution.py:37
  290.6 3.5 collective-permute-done.10
  295.9 3.7 collective-permute-start.11
  299.6 2.0 bitcast_add_fusion.3
  305.2 2.5 collective-permute-done.11
  309.5 3.7 collective-permute-start.12
  313.2 2.0 bitcast_add_fusion.4
  322.2 3.7 collective-permute-start.13
  325.9 2.0 bitcast_add_fusion.5
  328.7 3.4 collective-permute-done.13
  333.1 4.5 %collective-permute-done.6 = f32[296,384]{1,0:T(8,128)} collective-permute-done((f32[296,384]{1,0:T(8,128)}, f32[296,384]{1,0:T(8,128)}, u32[]{:S(2)}, u32[]{:S(2)}) %collective-permute-start.6) | collective-permute-done | bytes 454688 | tf_op jit(solution)/shard_map/ppermute | solution.py:37
  340.0 62.0 %psum.7 = f32[576]{0:T(1024)} all-reduce(f32[576]{0:T(1024)S(1)} %get-tuple-element.17), channel_id=1, replica_groups=mesh['dp'=32,'tensor'=8] {'dp'}, use_global_device_ids=true, to_apply=%region_8.9 | all-reduce | flops 576 | bytes 4608 | tf_op jit(solution)/shard_map/psum | solution.py:97
  (60 shorter events, 24.2 us)
Async XLA Ops:
  7.2 77.8 %all-gather.4.cloned.1.call-start = ((), (), s32[]{:S(2)}) async-start(), calls=%async_computation.1 | async-start | bytes 3981312 | tf_op jit(solution)/shard_map/all_gather | solution.py:48
  7.9 394.1 %reduce-scatter.2.cloned.1.call-start = ((), (), s32[]{:S(2)}) async-start(), calls=%async_computation.2 | async-start | bytes 19464192 | tf_op jit(solution)/shard_map/reduce_scatter | solution.py:64
  89.3 0.8 copy-start.6
  90.1 35.0 %copy-start.7 = (s32[384]{0:T(512)S(1)}, s32[384]{0:T(512)}, u32[]{:S(2)}) copy-start(s32[384]{0:T(512)} %param.11) | copy-start | bytes 4612
  96.8 28.3 %copy-start.3 = (f32[384,1024]{1,0:T(8,128)}, f32[384,1024]{1,0:T(8,128)S(1)}, u32[]{:S(2)}) copy-start(f32[384,1024]{1,0:T(8,128)S(1)} %get-tuple-element.37) | copy-start | bytes 4718596
  134.6 0.7 copy-start.5
  172.8 1.9 copy-start.1
  173.7 25.0 %collective-permute-start.7 = (f32[288,384]{1,0:T(8,128)}, f32[288,384]{1,0:T(8,128)}, u32[]{:S(2)}, u32[]{:S(2)}) collective-permute-start(f32[288,384]{1,0:T(8,128)} %dynamic-slice_bitcast_fusion.1), channel_id=1, source_target_pairs={{0,4},{1,0},{2,1},{3,2},{7,3},{6,7},{5,6},{4,5},{8,12},{9,8},{10,9... | collective-permute-start | bytes 1327112 | tf_op jit(solution)/shard_map/ppermute | solution.py:38
  174.7 1.9 copy-start
  177.4 96.0 %copy-start.2 = (f32[8,288,384]{2,1,0:T(8,128)S(1)}, f32[8,288,384]{2,1,0:T(8,128)}, u32[]{:S(2)}) copy-start(f32[8,288,384]{2,1,0:T(8,128)} %copy-done.1) | copy-start | bytes 10616836
  177.4 37.6 %collective-permute-start = (f32[296,384]{1,0:T(8,128)}, f32[296,384]{1,0:T(8,128)}, u32[]{:S(2)}, u32[]{:S(2)}) collective-permute-start(f32[296,384]{1,0:T(8,128)} %dynamic-slice_bitcast_fusion), channel_id=1, source_target_pairs={{0,1},{1,2},{2,3},{3,7},{7,6},{6,5},{5,4},{4,0},{8,9},{9,10},{10,1... | collective-permute-start | bytes 1363976 | tf_op jit(solution)/shard_map/ppermute | solution.py:37
  200.7 30.4 %collective-permute-start.8 = (f32[288,384]{1,0:T(8,128)}, f32[288,384]{1,0:T(8,128)}, u32[]{:S(2)}, u32[]{:S(2)}) collective-permute-start(f32[288,384]{1,0:T(8,128)} %bitcast_add_fusion.7), channel_id=1, source_target_pairs={{0,4},{1,0},{2,1},{3,2},{7,3},{6,7},{5,6},{4,5},{8,12},{9,8},{10,9... | collective-permute-start | bytes 1327112 | tf_op jit(solution)/shard_map/ppermute | solution.py:38
  217.0 32.6 %collective-permute-start.1 = (f32[296,384]{1,0:T(8,128)}, f32[296,384]{1,0:T(8,128)}, u32[]{:S(2)}, u32[]{:S(2)}) collective-permute-start(f32[296,384]{1,0:T(8,128)} %bitcast_add_fusion), channel_id=1, source_target_pairs={{0,1},{1,2},{2,3},{3,7},{7,6},{6,5},{5,4},{4,0},{8,9},{9,10},{10,1... | collective-permute-start | bytes 1363976 | tf_op jit(solution)/shard_map/ppermute | solution.py:37
  233.1 40.3 %collective-permute-start.9 = (f32[288,384]{1,0:T(8,128)}, f32[288,384]{1,0:T(8,128)}, u32[]{:S(2)}, u32[]{:S(2)}) collective-permute-start(f32[288,384]{1,0:T(8,128)} %bitcast_add_fusion.8), channel_id=1, source_target_pairs={{0,4},{1,0},{2,1},{3,2},{7,3},{6,7},{5,6},{4,5},{8,12},{9,8},{10,9... | collective-permute-start | bytes 1327112 | tf_op jit(solution)/shard_map/ppermute | solution.py:38
  251.6 33.1 %collective-permute-start.2 = (f32[296,384]{1,0:T(8,128)}, f32[296,384]{1,0:T(8,128)}, u32[]{:S(2)}, u32[]{:S(2)}) collective-permute-start(f32[296,384]{1,0:T(8,128)} %bitcast_add_fusion.1), channel_id=1, source_target_pairs={{0,1},{1,2},{2,3},{3,7},{7,6},{6,5},{5,4},{4,0},{8,9},{9,10},{10,1... | collective-permute-start | bytes 1363976 | tf_op jit(solution)/shard_map/ppermute | solution.py:37
  275.2 18.9 %collective-permute-start.10 = (f32[288,384]{1,0:T(8,128)}, f32[288,384]{1,0:T(8,128)}, u32[]{:S(2)}, u32[]{:S(2)}) collective-permute-start(f32[288,384]{1,0:T(8,128)} %bitcast_add_fusion.9), channel_id=1, source_target_pairs={{0,4},{1,0},{2,1},{3,2},{7,3},{6,7},{5,6},{4,5},{8,12},{9,8},{10,9... | collective-permute-start | bytes 1327112 | tf_op jit(solution)/shard_map/ppermute | solution.py:38
  286.7 13.0 %collective-permute-start.3 = (f32[296,384]{1,0:T(8,128)}, f32[296,384]{1,0:T(8,128)}, u32[]{:S(2)}, u32[]{:S(2)}) collective-permute-start(f32[296,384]{1,0:T(8,128)} %bitcast_add_fusion.2), channel_id=1, source_target_pairs={{0,1},{1,2},{2,3},{3,7},{7,6},{6,5},{5,4},{4,0},{8,9},{9,10},{10,1... | collective-permute-start | bytes 1363976 | tf_op jit(solution)/shard_map/ppermute | solution.py:37
  295.9 11.7 %collective-permute-start.11 = (f32[288,384]{1,0:T(8,128)}, f32[288,384]{1,0:T(8,128)}, u32[]{:S(2)}, u32[]{:S(2)}) collective-permute-start(f32[288,384]{1,0:T(8,128)} %bitcast_add_fusion.10), channel_id=1, source_target_pairs={{0,4},{1,0},{2,1},{3,2},{7,3},{6,7},{5,6},{4,5},{8,12},{9,8},{10,9... | collective-permute-start | bytes 1327112 | tf_op jit(solution)/shard_map/ppermute | solution.py:38
  301.6 11.6 %collective-permute-start.4 = (f32[296,384]{1,0:T(8,128)}, f32[296,384]{1,0:T(8,128)}, u32[]{:S(2)}, u32[]{:S(2)}) collective-permute-start(f32[296,384]{1,0:T(8,128)} %bitcast_add_fusion.3), channel_id=1, source_target_pairs={{0,1},{1,2},{2,3},{3,7},{7,6},{6,5},{5,4},{4,0},{8,9},{9,10},{10,1... | collective-permute-start | bytes 1363976 | tf_op jit(solution)/shard_map/ppermute | solution.py:37
  309.5 10.8 %collective-permute-start.12 = (f32[288,384]{1,0:T(8,128)}, f32[288,384]{1,0:T(8,128)}, u32[]{:S(2)}, u32[]{:S(2)}) collective-permute-start(f32[288,384]{1,0:T(8,128)} %bitcast_add_fusion.11), channel_id=1, source_target_pairs={{0,4},{1,0},{2,1},{3,2},{7,3},{6,7},{5,6},{4,5},{8,12},{9,8},{10,9... | collective-permute-start | bytes 1327112 | tf_op jit(solution)/shard_map/ppermute | solution.py:38
  315.2 10.7 %collective-permute-start.5 = (f32[296,384]{1,0:T(8,128)}, f32[296,384]{1,0:T(8,128)}, u32[]{:S(2)}, u32[]{:S(2)}) collective-permute-start(f32[296,384]{1,0:T(8,128)} %bitcast_add_fusion.4), channel_id=1, source_target_pairs={{0,1},{1,2},{2,3},{3,7},{7,6},{6,5},{5,4},{4,0},{8,9},{9,10},{10,1... | collective-permute-start | bytes 1363976 | tf_op jit(solution)/shard_map/ppermute | solution.py:37
  322.2 9.9 %collective-permute-start.13 = (f32[288,384]{1,0:T(8,128)}, f32[288,384]{1,0:T(8,128)}, u32[]{:S(2)}, u32[]{:S(2)}) collective-permute-start(f32[288,384]{1,0:T(8,128)} %bitcast_add_fusion.12), channel_id=1, source_target_pairs={{0,4},{1,0},{2,1},{3,2},{7,3},{6,7},{5,6},{4,5},{8,12},{9,8},{10,9... | collective-permute-start | bytes 1327112 | tf_op jit(solution)/shard_map/ppermute | solution.py:38
  327.8 9.8 %collective-permute-start.6 = (f32[296,384]{1,0:T(8,128)}, f32[296,384]{1,0:T(8,128)}, u32[]{:S(2)}, u32[]{:S(2)}) collective-permute-start(f32[296,384]{1,0:T(8,128)} %bitcast_add_fusion.5), channel_id=1, source_target_pairs={{0,1},{1,2},{2,3},{3,7},{7,6},{6,5},{5,4},{4,0},{8,9},{9,10},{10,1... | collective-permute-start | bytes 1363976 | tf_op jit(solution)/shard_map/ppermute | solution.py:37
  327.8 11.0 %copy-start.4 = (bf16[384,576]{0,1:T(8,128)(2,1)S(1)}, bf16[384,576]{0,1:T(8,128)(2,1)}, u32[]{:S(2)}) copy-start(bf16[384,576]{0,1:T(8,128)(2,1)} %param.8) | copy-start | bytes 1327108
Sparse Core Ops, SparseCore 0:
  10.6 74.3 all-gather.3
  134.7 149.8 reduce-scatter.1
where the time goes:
time: 410 us; the launch traced here: 409 us
  waiting for transfers between devices  161 us (39%)
  blocking collectives  89.8 us (22%)
  between operations  50.1 us (12%)
  starting transfers between devices  29.3 us (7%)
  other arithmetic  28.1 us (7%)
  matrix products  27.6 us (7%)
  local copies, waits for them, and re-layouts  22.9 us (6%)
    all_gather x1, waiting for transfers between devices, shards(): gathered = lax.all_gather(hidden_input_state, 'tensor', axis=1, tiled=True)  77 us
    psum x1, blocking collectives, shards(): lax.psum(jnp.sum(normed_gradient * normalized_slice, axis=0), 'dp')  62 us
    ppermute x7, waiting for transfers between devices, ring_reduce_scatter(): recv_b = lax.ppermute(send_b, axis, perm_b)  55.6 us
    ppermute x7, starting transfers between devices, ring_reduce_scatter(): recv_b = lax.ppermute(send_b, axis, perm_b)  28.5 us
    all_gather x1, blocking collectives, shards(): lax.all_gather(jnp.stack([local_top, local_total]), 'tensor', axis=0)  27.8 us
    ppermute x7, waiting for transfers between devices, ring_reduce_scatter(): recv_f = lax.ppermute(send_f, axis, perm_f)  27.7 us
    add x6, other arithmetic, ring_reduce_scatter(): send_f = send_f + recv_f  11.8 us
    dot_general x1, matrix products, shards(): lax.dot_general(head_weight, dlogits, (((1,), (1,)), ((), ())), preferred...  11.5 us
  transfers between devices with their start and end apart: 16, of which 12 were waited for; matrix products, arithmetic and copies ran while one was open for 13% of the time, Pallas kernels for 0%

commit v1 on v0

--- a/solution.py
+++ b/solution.py
@@ -94,7 +94,9 @@
     hidden_state_gradient = scaled_rows * (
         weighted_rows - normalized_slice * row_inner_sum[:, None]
     )
-    norm_gain_gradient = lax.psum(jnp.sum(normed_gradient * normalized_slice, axis=0), "dp")
+    norm_gain_gradient = jnp.sum(
+        lax.all_gather(jnp.sum(normed_gradient * normalized_slice, axis=0), "dp"), axis=0
+    )
     return (hidden_state_gradient, grad_head, norm_gain_gradient)
 
 

time: 410 us -> 611 us (1.49)
  waiting for transfers between devices: 161 us -> 436 us
  blocking collectives: 89.8 us -> 27.6 us
  starting transfers between devices: 29.3 us -> 11.4 us
    unnamed x2 -> x4, waiting for transfers between devices: 0.7 us -> 192 us
    reduce_scatter x1, waiting for transfers between devices: 0.01 us -> 148 us  [shards(): lax.psum_scatter(lax.dot_general(normed, dlogits, (((0,), (0,)), ((), ())...]
    psum x1 -> x0, blocking collectives: 62 us -> none  [shards(): lax.psum(jnp.sum(normed_gradient * normalized_slice, axis=0), 'dp')]
    ppermute x7, waiting for transfers between devices: 55.6 us -> 8.33 us  [ring_reduce_scatter(): recv_b = lax.ppermute(send_b, axis, perm_b)]
    ppermute x7, starting transfers between devices: 28.5 us -> 10.7 us  [ring_reduce_scatter(): recv_b = lax.ppermute(send_b, axis, perm_b)]
    all_gather x1, waiting for transfers between devices: 77 us -> 60.7 us  [shards(): gathered = lax.all_gather(hidden_input_state, 'tensor', axis=1, tiled=True)]
  transfers between devices with their start and end apart: 16 -> 17, of which waited for: 12 -> 15; matrix products, arithmetic and copies ran while one was open for 13% -> 7% of each run, Pallas kernels for 0% -> 0%
where the time goes in v1:
time: 611 us; the launch traced here: 608 us
  waiting for transfers between devices  436 us (71%)
  between operations  50.7 us (8%)
  other arithmetic  29.2 us (5%)
  local copies, waits for them, and re-layouts  27.6 us (5%)
  blocking collectives  27.6 us (5%)
  matrix products  24.7 us (4%)
  starting transfers between devices  11.4 us (2%)
    unnamed x4, waiting for transfers between devices  192 us
    reduce_scatter x1, waiting for transfers between devices, shards(): lax.psum_scatter(lax.dot_general(normed, dlogits, (((0,), (0,)), ((), ())...  148 us
    all_gather x1, waiting for transfers between devices, shards(): gathered = lax.all_gather(hidden_input_state, 'tensor', axis=1, tiled=True)  60.7 us
    all_gather x1, blocking collectives, shards(): lax.all_gather(jnp.stack([local_top, local_total]), 'tensor', axis=0)  27.6 us
    ppermute x7, waiting for transfers between devices, ring_reduce_scatter(): recv_f = lax.ppermute(send_f, axis, perm_f)  27.3 us
  transfers between devices with their start and end apart: 17, of which 15 were waited for; matrix products, arithmetic and copies ran while one was open for 7% of the time, Pallas kernels for 0%

profile of v1, /device:TPU:1, one launch (start us, length us, event | category | flops | bytes accessed | tf_op | source)
XLA Modules:
  0.0 607.5 jit_solution(16007585319517078657)
XLA Ops:
  18.5 1.9 fusion.16
  24.3 60.7 %all-gather.5.cloned.1.call-done = bf16[384,4608]{0,1:T(8,128)(2,1)} async-done(((bf16[384,576]{0,1:T(8,128)(2,1)}), bf16[384,4608]{0,1:T(8,128)(2,1)}) %all-gather.5.cloned.1.call-update) | async-done | bytes 3538960 | tf_op jit(solution)/shard_map/all_gather | solution.py:48
  85.0 4.3 copy.33
  90.2 7.0 %fusion.17 = (f32[384]{0:T(512)S(1)}, f32[384,1024]{1,0:T(8,128)S(1)}) fusion(bf16[4608,1024]{1,0:T(8,128)(2,1)} %param.10, bf16[384,4608]{1,0:T(8,128)(2,1)S(1)} %copy.33, f32[4608]{0:T(1024)S(1)} %copy-done.4, f32[384]{0:T(512)S(1)} %add_rsqrt_fusion), kind=kOutput, calls=%fused_computation.50 | convolution fusion | flops 3631349248 | bytes 14570496 | tf_op jit(solution)/shard_map/dot_general | solution.py:53
  97.6 27.6 %all-gather.2 = f32[8,2,384]{2,1,0:T(2,128)S(1)} all-gather(f32[1,2,384]{2,1,0:T(2,128)S(1)} %maximum_bitcast_fusion.1), channel_id=2, replica_groups=mesh['dp'=32,'tensor'=8] {'tensor'}, dimensions={0}, use_global_device_ids=true | all-gather | bytes 27648 | tf_op jit(solution)/shard_map/all_gather | solution.py:56
  125.4 6.8 %fusion.5 = (f32[384]{0:T(512)S(1)}, f32[4608,384]{0,1:T(8,128)}) fusion(bf16[384,4608]{1,0:T(8,128)(2,1)S(1)} %copy.33, f32[4608]{0:T(1024)S(1)} %copy-done.4, f32[384]{0:T(512)S(1)} %add_rsqrt_fusion, bf16[4608,1024]{1,0:T(8,128)(2,1)S(1)} %bitcast.94, f32[384,1024]{1,0:T(8,128)S(1)} %get-tuple-element.37, s32[1024]{0:T(1024)S(1)} %iota_add_fusion, ...), kind=kOutput, calls=%fused_computation.8 | convolution fusion | flops 3634691584 | bytes 21655552 | tf_op jit(solution)/shard_map/dot_general | solution.py:72
  132.2 8.0 %copy.35 = f32[4608,384]{1,0:T(8,128)} copy(f32[4608,384]{0,1:T(8,128)} %get-tuple-element.39) | data formatting | bytes 14155776 | tf_op jit(solution)/shard_map/dot_general | solution.py:72
  140.2 3.6 fusion.14
  152.7 2.0 bitcast_add_fusion.7
  154.7 2.3 collective-permute-start.8
  157.4 2.0 bitcast_add_fusion
  165.1 2.0 bitcast_add_fusion.8
  170.2 2.0 bitcast_add_fusion.1
  176.1 2.1 collective-permute-done.9
  178.2 2.0 bitcast_add_fusion.9
  181.1 3.0 collective-permute-done.2
  184.1 2.0 bitcast_add_fusion.2
  189.7 2.4 collective-permute-done.10
  192.1 2.0 bitcast_add_fusion.10
  195.0 4.0 collective-permute-done.3
  199.0 2.0 bitcast_add_fusion.3
  206.3 2.0 bitcast_add_fusion.11
  210.0 5.1 collective-permute-done.4
  215.1 2.0 bitcast_add_fusion.4
  220.9 2.0 bitcast_add_fusion.12
  222.9 3.0 collective-permute-start.13
  225.9 4.5 collective-permute-done.5
  230.3 2.0 bitcast_add_fusion.5
  236.1 8.6 %collective-permute-done.6 = f32[296,384]{1,0:T(8,128)} collective-permute-done((f32[296,384]{1,0:T(8,128)}, f32[296,384]{1,0:T(8,128)}, u32[]{:S(2)}, u32[]{:S(2)}) %collective-permute-start.6) | collective-permute-done | bytes 454688 | tf_op jit(solution)/shard_map/ppermute | solution.py:37
  249.2 10.9 %fusion.6 = f32[4608,1024]{1,0:T(8,128)} fusion(bf16[384,4608]{1,0:T(8,128)(2,1)S(1)} %copy.33, f32[4608]{0:T(1024)} %param.9, f32[384]{0:T(512)S(1)} %add_rsqrt_fusion, f32[384,1024]{1,0:T(8,128)} %copy-done.2, s32[1024]{0:T(1024)S(1)} %iota_add_fusion, f32[384]{0:T(512)S(1)} %log_add_fusion, s32[384]{0:T(512)} %param.11), kind=kOutput, calls=%fused_computation.13 | convolution fusion | flops 3632922624 | bytes 24013312 | tf_op jit(solution)/shard_map/dot_general | solution.py:65
  260.2 191.7 %all-reduce.4.cloned.1.call-done = f32[18432]{0:T(1024)} async-done(((f32[18432]{0:T(1024)}), f32[18432]{0:T(1024)}) %all-reduce.4.cloned.1.call-update) | async-done | bytes 73744
  453.4 147.6 %reduce-scatter.2.cloned.1.call-done = f32[144,1024]{1,0:T(8,128)} async-done(((f32[4608,1024]{1,0:T(8,128)}), f32[144,1024]{1,0:T(8,128)}) %reduce-scatter.2.cloned.1.call-update) | async-done | bytes 589840 | tf_op jit(solution)/shard_map/reduce_scatter | solution.py:64
  (72 shorter events, 28.1 us)
Async XLA Ops:
  7.2 77.8 %all-gather.5.cloned.1.call-start = ((), (), s32[]{:S(2)}) async-start(), calls=%async_computation.1 | async-start | bytes 3981312 | tf_op jit(solution)/shard_map/all_gather | solution.py:48
  7.9 444.0 %all-reduce.4.cloned.1.call-start = ((), (), s32[]{:S(2)}) async-start(), calls=%async_computation.3 | async-start | bytes 147456
  89.3 0.8 copy-start.4
  89.4 36.0 %slice-start = ((s8[9437184]{0:T(1024)(128)(4,1)}), s8[4194304]{0:T(1024)(128)(4,1)S(1)}, s32[]{:S(2)}) async-start(s8[9437184]{0:T(1024)(128)(4,1)} %bitcast.93), calls=%async_computation.4 | async-start | bytes 8388608
  90.2 35.2 %copy-start.5 = (s32[384]{0:T(512)S(1)}, s32[384]{0:T(512)}, u32[]{:S(2)}) copy-start(s32[384]{0:T(512)} %param.11) | copy-start | bytes 4612
  90.2 35.2 %slice-start.1 = ((s8[9437184]{0:T(1024)(128)(4,1)}), s8[4194304]{0:T(1024)(128)(4,1)S(1)}, s32[]{:S(2)}) async-start(s8[9437184]{0:T(1024)(128)(4,1)} %bitcast.93), calls=%async_computation.5 | async-start | bytes 8388608
  90.2 35.2 %slice-start.2 = ((s8[9437184]{0:T(1024)(128)(4,1)}), s8[1048576]{0:T(1024)(128)(4,1)S(1)}, s32[]{:S(2)}) async-start(s8[9437184]{0:T(1024)(128)(4,1)} %bitcast.93), calls=%async_computation.6 | async-start | bytes 2097152
  97.2 35.0 %copy-start.2 = (f32[384,1024]{1,0:T(8,128)}, f32[384,1024]{1,0:T(8,128)S(1)}, u32[]{:S(2)}) copy-start(f32[384,1024]{1,0:T(8,128)S(1)} %get-tuple-element.37) | copy-start | bytes 4718596
  143.8 2.0 copy-start.1
  144.7 8.1 %collective-permute-start.7 = (f32[288,384]{1,0:T(8,128)}, f32[288,384]{1,0:T(8,128)}, u32[]{:S(2)}, u32[]{:S(2)}) collective-permute-start(f32[288,384]{1,0:T(8,128)} %dynamic-slice_bitcast_fusion.1), channel_id=1, source_target_pairs={{0,4},{1,0},{2,1},{3,2},{7,3},{6,7},{5,6},{4,5},{8,12},{9,8},{10,9... | collective-permute-start | bytes 1327112 | tf_op jit(solution)/shard_map/ppermute | solution.py:38
  145.8 1.8 copy-start
  148.3 9.1 %collective-permute-start = (f32[296,384]{1,0:T(8,128)}, f32[296,384]{1,0:T(8,128)}, u32[]{:S(2)}, u32[]{:S(2)}) collective-permute-start(f32[296,384]{1,0:T(8,128)} %dynamic-slice_bitcast_fusion), channel_id=1, source_target_pairs={{0,1},{1,2},{2,3},{3,7},{7,6},{6,5},{5,4},{4,0},{8,9},{9,10},{10,1... | collective-permute-start | bytes 1363976 | tf_op jit(solution)/shard_map/ppermute | solution.py:37
  154.7 10.4 %collective-permute-start.8 = (f32[288,384]{1,0:T(8,128)}, f32[288,384]{1,0:T(8,128)}, u32[]{:S(2)}, u32[]{:S(2)}) collective-permute-start(f32[288,384]{1,0:T(8,128)} %bitcast_add_fusion.7), channel_id=1, source_target_pairs={{0,4},{1,0},{2,1},{3,2},{7,3},{6,7},{5,6},{4,5},{8,12},{9,8},{10,9... | collective-permute-start | bytes 1327112 | tf_op jit(solution)/shard_map/ppermute | solution.py:38
  159.4 10.8 %collective-permute-start.1 = (f32[296,384]{1,0:T(8,128)}, f32[296,384]{1,0:T(8,128)}, u32[]{:S(2)}, u32[]{:S(2)}) collective-permute-start(f32[296,384]{1,0:T(8,128)} %bitcast_add_fusion), channel_id=1, source_target_pairs={{0,1},{1,2},{2,3},{3,7},{7,6},{6,5},{5,4},{4,0},{8,9},{9,10},{10,1... | collective-permute-start | bytes 1363976 | tf_op jit(solution)/shard_map/ppermute | solution.py:37
  167.0 11.2 %collective-permute-start.9 = (f32[288,384]{1,0:T(8,128)}, f32[288,384]{1,0:T(8,128)}, u32[]{:S(2)}, u32[]{:S(2)}) collective-permute-start(f32[288,384]{1,0:T(8,128)} %bitcast_add_fusion.8), channel_id=1, source_target_pairs={{0,4},{1,0},{2,1},{3,2},{7,3},{6,7},{5,6},{4,5},{8,12},{9,8},{10,9... | collective-permute-start | bytes 1327112 | tf_op jit(solution)/shard_map/ppermute | solution.py:38
  172.2 11.9 %collective-permute-start.2 = (f32[296,384]{1,0:T(8,128)}, f32[296,384]{1,0:T(8,128)}, u32[]{:S(2)}, u32[]{:S(2)}) collective-permute-start(f32[296,384]{1,0:T(8,128)} %bitcast_add_fusion.1), channel_id=1, source_target_pairs={{0,1},{1,2},{2,3},{3,7},{7,6},{6,5},{5,4},{4,0},{8,9},{9,10},{10,1... | collective-permute-start | bytes 1363976 | tf_op jit(solution)/shard_map/ppermute | solution.py:37
  180.1 12.0 %collective-permute-start.10 = (f32[288,384]{1,0:T(8,128)}, f32[288,384]{1,0:T(8,128)}, u32[]{:S(2)}, u32[]{:S(2)}) collective-permute-start(f32[288,384]{1,0:T(8,128)} %bitcast_add_fusion.9), channel_id=1, source_target_pairs={{0,4},{1,0},{2,1},{3,2},{7,3},{6,7},{5,6},{4,5},{8,12},{9,8},{10,9... | collective-permute-start | bytes 1327112 | tf_op jit(solution)/shard_map/ppermute | solution.py:38
  186.0 13.0 %collective-permute-start.3 = (f32[296,384]{1,0:T(8,128)}, f32[296,384]{1,0:T(8,128)}, u32[]{:S(2)}, u32[]{:S(2)}) collective-permute-start(f32[296,384]{1,0:T(8,128)} %bitcast_add_fusion.2), channel_id=1, source_target_pairs={{0,1},{1,2},{2,3},{3,7},{7,6},{6,5},{5,4},{4,0},{8,9},{9,10},{10,1... | collective-permute-start | bytes 1363976 | tf_op jit(solution)/shard_map/ppermute | solution.py:37
  194.0 39.1 %copy-start.6 = (u32[256]{0:T(256)S(1)}, u32[256]{0:T(256)}, u32[]{:S(2)}) copy-start(u32[256]{0:T(256)} %constant.209) | copy-start | bytes 3076
  194.0 12.2 %collective-permute-start.11 = (f32[288,384]{1,0:T(8,128)}, f32[288,384]{1,0:T(8,128)}, u32[]{:S(2)}, u32[]{:S(2)}) collective-permute-start(f32[288,384]{1,0:T(8,128)} %bitcast_add_fusion.10), channel_id=1, source_target_pairs={{0,4},{1,0},{2,1},{3,2},{7,3},{6,7},{5,6},{4,5},{8,12},{9,8},{10,9... | collective-permute-start | bytes 1327112 | tf_op jit(solution)/shard_map/ppermute | solution.py:38
  201.0 14.1 %collective-permute-start.4 = (f32[296,384]{1,0:T(8,128)}, f32[296,384]{1,0:T(8,128)}, u32[]{:S(2)}, u32[]{:S(2)}) collective-permute-start(f32[296,384]{1,0:T(8,128)} %bitcast_add_fusion.3), channel_id=1, source_target_pairs={{0,1},{1,2},{2,3},{3,7},{7,6},{6,5},{5,4},{4,0},{8,9},{9,10},{10,1... | collective-permute-start | bytes 1363976 | tf_op jit(solution)/shard_map/ppermute | solution.py:37
  208.2 12.7 %collective-permute-start.12 = (f32[288,384]{1,0:T(8,128)}, f32[288,384]{1,0:T(8,128)}, u32[]{:S(2)}, u32[]{:S(2)}) collective-permute-start(f32[288,384]{1,0:T(8,128)} %bitcast_add_fusion.11), channel_id=1, source_target_pairs={{0,4},{1,0},{2,1},{3,2},{7,3},{6,7},{5,6},{4,5},{8,12},{9,8},{10,9... | collective-permute-start | bytes 1327112 | tf_op jit(solution)/shard_map/ppermute | solution.py:38
  217.1 13.3 %collective-permute-start.5 = (f32[296,384]{1,0:T(8,128)}, f32[296,384]{1,0:T(8,128)}, u32[]{:S(2)}, u32[]{:S(2)}) collective-permute-start(f32[296,384]{1,0:T(8,128)} %bitcast_add_fusion.4), channel_id=1, source_target_pairs={{0,1},{1,2},{2,3},{3,7},{7,6},{6,5},{5,4},{4,0},{8,9},{9,10},{10,1... | collective-permute-start | bytes 1363976 | tf_op jit(solution)/shard_map/ppermute | solution.py:37
  222.9 12.0 %collective-permute-start.13 = (f32[288,384]{1,0:T(8,128)}, f32[288,384]{1,0:T(8,128)}, u32[]{:S(2)}, u32[]{:S(2)}) collective-permute-start(f32[288,384]{1,0:T(8,128)} %bitcast_add_fusion.12), channel_id=1, source_target_pairs={{0,4},{1,0},{2,1},{3,2},{7,3},{6,7},{5,6},{4,5},{8,12},{9,8},{10,9... | collective-permute-start | bytes 1327112 | tf_op jit(solution)/shard_map/ppermute | solution.py:38
  232.3 12.4 %collective-permute-start.6 = (f32[296,384]{1,0:T(8,128)}, f32[296,384]{1,0:T(8,128)}, u32[]{:S(2)}, u32[]{:S(2)}) collective-permute-start(f32[296,384]{1,0:T(8,128)} %bitcast_add_fusion.5), channel_id=1, source_target_pairs={{0,1},{1,2},{2,3},{3,7},{7,6},{6,5},{5,4},{4,0},{8,9},{9,10},{10,1... | collective-permute-start | bytes 1363976 | tf_op jit(solution)/shard_map/ppermute | solution.py:37
  232.3 13.6 %copy-start.3 = (bf16[384,576]{0,1:T(8,128)(2,1)S(1)}, bf16[384,576]{0,1:T(8,128)(2,1)}, u32[]{:S(2)}) copy-start(bf16[384,576]{0,1:T(8,128)(2,1)} %param.8) | copy-start | bytes 1327108
  249.2 351.8 %reduce-scatter.2.cloned.1.call-start = ((), (), s32[]{:S(2)}) async-start(), calls=%async_computation.2 | async-start | bytes 19464192 | tf_op jit(solution)/shard_map/reduce_scatter | solution.py:64
Sparse Core Ops, SparseCore 0:
  10.6 74.3 all-gather.4
  249.3 202.5 all-reduce.3
  455.2 145.7 reduce-scatter.1
